TPU v7x, 512 devices: a whole 4x4x16 slice. The times are simulated.
512 devices in a mesh: row: 64 (over x_lo, z, core), col: 8 (over y, x_hi).
Axes of the slice: x: 4 (x_hi: 2, x_lo: 2; x = x_hi * 2 + x_lo), y: 4, z: 16, core: 2. Of those that a mesh axis runs over, the one named last changes fastest.
Arguments:
- features: bfloat16 [128, 131072], P(None, 'row'), may hold values from -6 to 6
- weight_in: bfloat16 [128, 512], P(None, 'col'), may hold values from -0.5 to 0.5
- weight_out: bfloat16 [512, 64], replicated, may hold values from -0.25 to 0.25
- score_grad: bfloat16 [64, 131072], P('col', 'row'), may hold values from -0.011962891 to 0.011962891
- band_blocks: bfloat16 [1024, 3, 128, 128], P('row'), may hold values from -0.25 to 0.25
- long_blocks: bfloat16 [768, 128, 128], P('row'), may hold values from -0.25 to 0.25
- long_rows: int32 [64, 12], P('row'), may hold values from 0 to 15
- long_sources: int32 [64, 12], replicated, may hold values from 0 to 1023, as said below
- long_counts: int32 [64], replicated, may hold values from 1 to 12, as said below
Outputs:
- scores: bfloat16 [64, 131072], P('col', 'row')
- first_grad: float32 [128, 512], P(None, 'col')
- second_grad: float32 [512, 64], P('col')
Inputs may be any that keep to these rules, and one draw needn't show every extreme that they name: `long_sources`: every slot's block column lies on a partition at cycle distance 1 to 3 from the slot's own partition (either direction, indices taken mod the number of partitions); over ALL 12 slots of a partition each of the 6 such partitions is read by exactly 2 slots. Slots s < long_counts[p] are live, the others are ignored; some partition has all 12 live.
All inputs are finite; a program needn't handle non-finite values.
Results may differ from a plain program's by a relative error of at most 0.0065.
Values may be sent and summed in bfloat16 or wider, within the bound.
No kernel may reach another device: no remote copies, remote signals or barrier semaphores. Data moves between devices by JAX's collectives and lax.ppermute only.
A program may use at most 64 MiB of HBM per device.

v0:
```python
import jax
import jax.numpy as jnp
from jax import lax
from jax.sharding import PartitionSpec as P

BLK = 128
NB = 16
REACH = 3
SLOTS = 12


def passed_along(x, axis, by):
    devices = lax.axis_size(axis)
    return lax.ppermute(x, axis, [(i, (i + by) % devices) for i in range(devices)])


def signed_offset(owner_part, partition, row_devices):
    offset = jnp.mod(owner_part - partition, row_devices)
    return jnp.where(offset > row_devices // 2, offset - row_devices, offset)


def slot_table(long_sources, long_counts, partition, row_devices):
    source = lax.dynamic_index_in_dim(long_sources, partition, 0, keepdims=False)
    live_count = lax.dynamic_index_in_dim(long_counts, partition, 0, keepdims=False)
    slot_order = jnp.arange(SLOTS, dtype=jnp.int32)
    is_live = slot_order < live_count
    owner_part = source // NB
    local_block = source - owner_part * NB
    offset = signed_offset(owner_part, partition, row_devices)
    same_offset = (
        (offset[:, None] == offset[None, :])
        & is_live[None, :]
        & (slot_order[None, :] < slot_order[:, None])
    )
    slot_rank = jnp.sum(same_offset.astype(jnp.int32), axis=1)
    return (is_live, offset, local_block, slot_rank)


def distances():
    return [distance for distance in range(-REACH, REACH + 1) if distance != 0]


def aggregate(values, band_blocks, long_blocks, row_ids, long_sources, long_counts):
    feature_rows = values.shape[0]
    row_devices = lax.axis_size("row")
    my_index = lax.axis_index("row")
    blocks = values.reshape(feature_rows, NB, BLK)
    is_live, offset, local_block, slot_rank = slot_table(
        long_sources, long_counts, my_index, row_devices
    )
    position = jnp.where(offset < 0, offset + REACH, offset + REACH - 1)
    received = {}
    for distance in distances():
        arrived = passed_along(values, "row", -distance)
        received[distance] = arrived.reshape(feature_rows, NB, BLK)
    panel_pool = jnp.stack([received[distance] for distance in distances()], 0)
    panel_pool = panel_pool.transpose(0, 2, 1, 3).reshape(2 * REACH * NB, feature_rows, BLK)
    slot_index = position * NB + local_block
    before = received[-1][:, NB - 1]
    beyond = received[1][:, 0]
    slot_index = jnp.clip(slot_index, 0, panel_pool.shape[0] - 1)
    panels = jnp.take(panel_pool, slot_index, axis=0)
    contrib = jnp.einsum("kfm,knm->kfn", panels, long_blocks, preferred_element_type=jnp.float32)
    contrib = contrib * is_live.astype(jnp.float32)[:, None, None]
    targets = (
        (row_ids[:, None] == jnp.arange(NB, dtype=jnp.int32)[None, :]) & is_live[:, None]
    ).astype(jnp.float32)
    far_sum = jnp.einsum("kb,kfn->fbn", targets, contrib, precision=lax.Precision.HIGHEST)
    earlier = jnp.concatenate([before[:, None], blocks[:, :-1]], 1)
    onward = jnp.concatenate([blocks[:, 1:], beyond[:, None]], 1)
    near_sum = jnp.einsum(
        "fbm,bnm->fbn", earlier, band_blocks[:, 0], preferred_element_type=jnp.float32
    )
    near_sum = near_sum + jnp.einsum(
        "fbm,bnm->fbn", blocks, band_blocks[:, 1], preferred_element_type=jnp.float32
    )
    near_sum = near_sum + jnp.einsum(
        "fbm,bnm->fbn", onward, band_blocks[:, 2], preferred_element_type=jnp.float32
    )
    return (near_sum + far_sum).reshape(feature_rows, NB * BLK)


def aggregate_back(values, band_blocks, long_blocks, row_ids, long_sources, long_counts):
    feature_rows = values.shape[0]
    row_devices = lax.axis_size("row")
    my_index = lax.axis_index("row")
    blocks = values.reshape(feature_rows, NB, BLK)
    is_live, offset, local_block, slot_rank = slot_table(
        long_sources, long_counts, my_index, row_devices
    )
    to_prior = jnp.einsum(
        "fbn,bnm->fbm", blocks, band_blocks[:, 0], preferred_element_type=jnp.float32
    )
    middle = jnp.einsum(
        "fbn,bnm->fbm", blocks, band_blocks[:, 1], preferred_element_type=jnp.float32
    )
    to_later = jnp.einsum(
        "fbn,bnm->fbm", blocks, band_blocks[:, 2], preferred_element_type=jnp.float32
    )
    zero_block = jnp.zeros((feature_rows, 1, BLK), jnp.float32)
    summed = (
        middle
        + jnp.concatenate([to_prior[:, 1:], zero_block], 1)
        + jnp.concatenate([zero_block, to_later[:, :-1]], 1)
    )
    edge_prior = to_prior[:, 0]
    edge_later = to_later[:, NB - 1]
    gathered_rows = jnp.take(blocks, row_ids, axis=1)
    contrib = jnp.einsum(
        "fkn,knm->kfm", gathered_rows, long_blocks, preferred_element_type=jnp.float32
    )
    contrib = contrib * is_live.astype(jnp.float32)[:, None, None]
    block_hot = local_block[:, None] == jnp.arange(NB, dtype=jnp.int32)[None, :]
    for distance in distances():
        placing = ((is_live & (offset == distance))[:, None] & block_hot).astype(jnp.float32)
        outgoing = jnp.einsum("kb,kfm->fbm", placing, contrib, precision=lax.Precision.HIGHEST)
        if distance == -1:
            outgoing = outgoing.at[:, NB - 1].add(edge_prior)
        if distance == 1:
            outgoing = outgoing.at[:, 0].add(edge_later)
        summed = summed + passed_along(outgoing, "row", distance)
    return summed.reshape(feature_rows, NB * BLK)


def local(
    features,
    weight_in,
    weight_out,
    score_grad,
    band_blocks,
    long_blocks,
    long_rows,
    long_sources,
    long_counts,
):
    row_ids = long_rows[0]
    hidden_count = weight_in.shape[1]
    class_count = score_grad.shape[0]
    col_index = lax.axis_index("col")
    my_rows = lax.dynamic_slice_in_dim(weight_out, col_index * hidden_count, hidden_count, 0)
    hidden_in = jnp.einsum(
        "ih,in->hn", weight_in, features, preferred_element_type=jnp.float32
    ).astype(jnp.bfloat16)
    hidden_sum = aggregate(hidden_in, band_blocks, long_blocks, row_ids, long_sources, long_counts)
    hidden_act = jax.nn.silu(hidden_sum).astype(jnp.bfloat16)
    out_cols = lax.dynamic_slice_in_dim(weight_out, col_index * class_count, class_count, 1)
    class_sum = jnp.einsum(
        "hc,hn->cn",
        out_cols,
        lax.all_gather(hidden_act, "col", axis=0, tiled=True),
        preferred_element_type=jnp.float32,
    )
    class_in = class_sum.astype(jnp.bfloat16)
    scores = aggregate(
        class_in, band_blocks, long_blocks, row_ids, long_sources, long_counts
    ).astype(jnp.bfloat16)
    class_back = aggregate_back(
        score_grad, band_blocks, long_blocks, row_ids, long_sources, long_counts
    ).astype(jnp.bfloat16)
    shard_piece = lax.all_gather(class_back, "col", axis=0, tiled=True)
    hidden_back = jnp.einsum("hc,cn->hn", my_rows, shard_piece, preferred_element_type=jnp.float32)
    block_grad = jnp.einsum(
        "hn,cn->hc", hidden_act, shard_piece, preferred_element_type=jnp.float32
    )
    second_part = block_grad
    hidden_back, second_part = (hidden_back, second_part)
    sigmoid_val = jax.nn.sigmoid(hidden_sum)
    slope_back = (hidden_back * sigmoid_val * (1.0 + hidden_sum * (1.0 - sigmoid_val))).astype(
        jnp.bfloat16
    )
    input_back = aggregate_back(
        slope_back, band_blocks, long_blocks, row_ids, long_sources, long_counts
    ).astype(jnp.bfloat16)
    first_part = jnp.einsum("in,hn->ih", features, input_back, preferred_element_type=jnp.float32)
    first_grad, second_grad = lax.psum((first_part, second_part), "row")
    return (scores, first_grad, second_grad)


def solution(mesh):
    return jax.shard_map(
        local,
        mesh=mesh,
        in_specs=(
            P(None, "row"),
            P(None, "col"),
            P(),
            P("col", "row"),
            P("row", None, None, None),
            P("row", None, None),
            P("row", None),
            P(),
            P(),
        ),
        out_specs=(P("col", "row"), P(None, "col"), P("col", None)),
        check_vma=False,
    )
```

profile of v0, /device:TPU:2, one launch (start us, length us, event | category | flops | bytes accessed | tf_op | source)
XLA Modules:
  0.0 423.3 jit_solution(10532549555107713151)
XLA Ops:
  7.3 1.4 dynamic_slice.22
  11.6 1.3 compare_and_fusion.4
  13.0 1.3 gather_fusion.2
  14.3 1.3 convolution_multiply_fusion.3
  15.8 3.3 collective-permute-start.17
  19.3 3.8 collective-permute-start.16
  23.9 1.3 convolution_bitcast_fusion.3
  25.8 3.6 collective-permute-start.15
  31.2 5.8 %collective-permute-start.14 = (f32[8,16,128]{2,0,1:T(8,128)}, f32[8,16,128]{2,0,1:T(8,128)S(1)}, u32[]{:S(2)}, u32[]{:S(2)}) collective-permute-start(f32[8,16,128]{2,0,1:T(8,128)} %fusion.150), channel_id=1, source_target_pairs={{0,504},{8,0},{16,8},{24,16},{32,24},{40,32},{48,40},{56,48},{64,5... | collective-permute-start | bytes 196616 | tf_op jit(solution)/shard_map/ppermute | solution.py:14
  37.3 4.2 collective-permute-start.13
  42.8 3.1 collective-permute-start.12
  46.0 2.9 collective-permute-start
  48.8 1.9 collective-permute-start.2
  50.8 1.9 collective-permute-start.3
  52.7 5.4 %collective-permute-start.1 = (bf16[64,2048]{1,0:T(8,128)(2,1)S(1)}, bf16[64,2048]{1,0:T(8,128)(2,1)S(1)}, u32[]{:S(2)}, u32[]{:S(2)}) collective-permute-start(bf16[64,2048]{1,0:T(8,128)(2,1)S(1)} %convolution_convert_fusion), channel_id=1, source_target_pairs={{0,504},{8,0},{16,8},{24,16},{32,24},{40,32},{48,40},{56,48},{64,5... | collective-permute-start | bytes 786440 | tf_op jit(solution)/shard_map/ppermute | solution.py:14
  58.1 3.8 collective-permute-start.4
  62.1 41.0 %all_gather.7 = bf16[64,2048]{1,0:T(8,128)(2,1)} all-gather(bf16[8,2048]{1,0:T(8,128)(2,1)S(1)} %fusion.27), channel_id=1, replica_groups=mesh['row'=64,'col'=8] {'col'}, dimensions={0}, use_global_device_ids=true | all-gather | bytes 294912 | tf_op jit(solution)/shard_map/all_gather | solution.py:160
  103.1 1.9 collective-permute-start.5
  106.4 6.8 %collective-permute-done.5 = bf16[64,2048]{1,0:T(8,128)(2,1)S(1)} collective-permute-done((bf16[64,2048]{1,0:T(8,128)(2,1)S(1)}, bf16[64,2048]{1,0:T(8,128)(2,1)S(1)}, u32[]{:S(2)}, u32[]{:S(2)}) %collective-permute-start.5) | collective-permute-done | bytes 262176 | tf_op jit(solution)/shard_map/ppermute | solution.py:14
  114.4 1.2 copy-done.7
  115.5 2.0 gather_fusion
  118.7 1.4 fusion.12
  121.0 1.4 fusion.15
  123.1 0.9 convolution_multiply_fusion.1
  124.9 1.9 collective-permute-start.23
  127.5 1.0 copy.189
  128.5 1.9 collective-permute-start.22
  133.1 2.1 collective-permute-start.21
  137.8 5.5 %collective-permute-start.20 = (f32[64,16,128]{2,0,1:T(8,128)}, f32[64,16,128]{2,0,1:T(8,128)}, u32[]{:S(2)}, u32[]{:S(2)}) collective-permute-start(f32[64,16,128]{2,0,1:T(8,128)} %fusion.105), channel_id=1, source_target_pairs={{0,504},{8,0},{16,8},{24,16},{32,24},{40,32},{48,40},{56,48},{64,5... | collective-permute-start | bytes 1572872 | tf_op jit(solution)/shard_map/ppermute | solution.py:14
  144.1 1.0 copy.190
  145.8 4.6 %collective-permute-start.19 = (f32[64,16,128]{2,0,1:T(8,128)}, f32[64,16,128]{2,0,1:T(8,128)}, u32[]{:S(2)}, u32[]{:S(2)}) collective-permute-start(f32[64,16,128]{2,0,1:T(8,128)} %bitcast.315), channel_id=1, source_target_pairs={{0,496},{8,504},{16,0},{24,8},{32,16},{40,24},{48,32},{56,40},{64,... | collective-permute-start | bytes 1572872 | tf_op jit(solution)/shard_map/ppermute | solution.py:14
  150.4 1.0 copy.191
  151.4 3.3 collective-permute-start.18
  154.7 0.9 copy-done.6
  155.9 5.4 %collective-permute-done.22 = f32[64,16,128]{2,0,1:T(8,128)} collective-permute-done((f32[64,16,128]{2,0,1:T(8,128)}, f32[64,16,128]{2,0,1:T(8,128)}, u32[]{:S(2)}, u32[]{:S(2)}) %collective-permute-start.22) | collective-permute-done | bytes 524320 | tf_op jit(solution)/shard_map/ppermute | solution.py:14
  161.2 2.5 collective-permute-done.21
  163.7 14.8 %collective-permute-done.18 = f32[64,16,128]{2,0,1:T(8,128)} collective-permute-done((f32[64,16,128]{2,0,1:T(8,128)}, f32[64,16,128]{2,0,1:T(8,128)}, u32[]{:S(2)}, u32[]{:S(2)}) %collective-permute-start.18) | collective-permute-done | bytes 524320 | tf_op jit(solution)/shard_map/ppermute | solution.py:14
  178.5 2.2 fusion.14
  181.0 209.5 %all-reduce.4 = (f32[128,64]{0,1:T(8,128)}, f32[64,64]{1,0:T(8,128)}) all-reduce(f32[128,64]{0,1:T(8,128)S(1)} %convolution_bitcast_fusion.6, f32[64,64]{1,0:T(8,128)S(1)} %fusion.208), channel_id=1, replica_groups=mesh['row'=64,'col'=8] {'row'}, use_global_device_ids=true, to_apply=%region_0.1 | all-reduce | flops 12288 | bytes 98304 | tf_op jit(solution)/shard_map/psum | solution.py:175
  390.6 2.0 convolution_convert_fusion.1
  392.9 1.9 collective-permute-start.6
  394.9 1.9 collective-permute-start.8
  396.8 1.9 collective-permute-start.9
  398.7 5.8 %collective-permute-start.7 = (bf16[8,2048]{1,0:T(8,128)(2,1)S(1)}, bf16[8,2048]{1,0:T(8,128)(2,1)S(1)}, u32[]{:S(2)}, u32[]{:S(2)}) collective-permute-start(bf16[8,2048]{1,0:T(8,128)(2,1)S(1)} %convolution_convert_fusion.1), channel_id=1, source_target_pairs={{0,504},{8,0},{16,8},{24,16},{32,24},{40,32},{48,40},{56,48},{64,5... | collective-permute-start | bytes 98312 | tf_op jit(solution)/shard_map/ppermute | solution.py:14
  404.5 3.6 collective-permute-start.10
  408.2 3.5 collective-permute-start.11
  411.8 2.2 collective-permute-done.11
  415.5 1.0 fusion.29
  (165 shorter events, 23.9 us)
Async XLA Ops:
  7.2 34.3 %copy-start = (bf16[128,2048]{1,0:T(8,128)(2,1)S(1)}, bf16[128,2048]{1,0:T(8,128)(2,1)}, u32[]{:S(2)}) copy-start(bf16[128,2048]{1,0:T(8,128)(2,1)} %param.17) | copy-start | bytes 1572868
  7.2 22.3 %copy-start.8 = (bf16[8,2048]{1,0:T(8,128)(2,1)S(1)}, bf16[8,2048]{1,0:T(8,128)(2,1)}, u32[]{:S(2)}) copy-start(bf16[8,2048]{1,0:T(8,128)(2,1)} %param.20) | copy-start | bytes 98308
  7.2 22.3 %copy-start.1 = (bf16[16,3,128,128]{3,2,1,0:T(8,128)(2,1)S(1)}, bf16[16,3,128,128]{3,2,1,0:T(8,128)(2,1)}, u32[]{:S(2)}) copy-start(bf16[16,3,128,128]{3,2,1,0:T(8,128)(2,1)} %param.21) | copy-start | bytes 4718596
  7.2 383.3 %all-gather.2.cloned.1.call-start = ((), (), s32[]{:S(2)}) async-start(), calls=%async_computation | async-start | bytes 2359296 | tf_op jit(solution)/shard_map/all_gather | solution.py:150
  9.3 108.7 %copy-start.27 = (pred[12]{0:T(512)(128)(4,1)}, pred[12]{0:T(512)(128)(4,1)S(1)}, u32[]{:S(2)}) copy-start(pred[12]{0:T(512)(128)(4,1)S(1)} %get-tuple-element.80) | copy-start | bytes 40
  10.9 31.7 %copy-start.12 = (pred[12]{0:T(512)(128)(4,1)}, pred[12]{0:T(512)(128)(4,1)S(1)}, u32[]{:S(2)}) copy-start(pred[12]{0:T(512)(128)(4,1)S(1)} %get-tuple-element.53) | copy-start | bytes 40
  11.6 18.4 %copy-start.11 = (s32[1024]{0:T(1024)}, s32[1024]{0:T(1024)S(1)}, u32[]{:S(2)}) copy-start(s32[1024]{0:T(1024)S(1)} %pad_clamp_fusion) | copy-start | bytes 12292
  12.9 17.1 %copy-start.16 = (pred[12]{0:T(512)(128)(4,1)}, pred[12]{0:T(512)(128)(4,1)S(1)}, u32[]{:S(2)}) copy-start(pred[12]{0:T(512)(128)(4,1)S(1)} %get-tuple-element.71) | copy-start | bytes 40
  12.9 17.1 %copy-start.18 = (pred[12]{0:T(512)(128)(4,1)}, pred[12]{0:T(512)(128)(4,1)S(1)}, u32[]{:S(2)}) copy-start(pred[12]{0:T(512)(128)(4,1)S(1)} %get-tuple-element.72) | copy-start | bytes 40
  12.9 17.1 %copy-start.20 = (pred[12]{0:T(512)(128)(4,1)}, pred[12]{0:T(512)(128)(4,1)S(1)}, u32[]{:S(2)}) copy-start(pred[12]{0:T(512)(128)(4,1)S(1)} %get-tuple-element.74) | copy-start | bytes 40
  12.9 17.1 %copy-start.22 = (pred[12]{0:T(512)(128)(4,1)}, pred[12]{0:T(512)(128)(4,1)S(1)}, u32[]{:S(2)}) copy-start(pred[12]{0:T(512)(128)(4,1)S(1)} %get-tuple-element.73) | copy-start | bytes 40
  12.9 17.1 %copy-start.26 = (pred[12]{0:T(512)(128)(4,1)}, pred[12]{0:T(512)(128)(4,1)S(1)}, u32[]{:S(2)}) copy-start(pred[12]{0:T(512)(128)(4,1)S(1)} %get-tuple-element.77) | copy-start | bytes 40
  12.9 24.1 %copy-start.14 = (pred[12]{0:T(512)(128)(4,1)}, pred[12]{0:T(512)(128)(4,1)S(1)}, u32[]{:S(2)}) copy-start(pred[12]{0:T(512)(128)(4,1)S(1)} %get-tuple-element.70) | copy-start | bytes 40
  13.0 104.6 %copy-start.24 = (pred[12]{0:T(512)(128)(4,1)}, pred[12]{0:T(512)(128)(4,1)S(1)}, u32[]{:S(2)}) copy-start(pred[12]{0:T(512)(128)(4,1)S(1)} %get-tuple-element.75) | copy-start | bytes 40
  15.6 25.9 %copy-start.9 = (bf16[128,64]{0,1:T(8,128)(2,1)S(1)}, bf16[128,64]{0,1:T(8,128)(2,1)}, u32[]{:S(2)}) copy-start(bf16[128,64]{0,1:T(8,128)(2,1)} %param.18) | copy-start | bytes 49156
  15.8 27.1 %collective-permute-start.17 = (f32[8,16,128]{2,0,1:T(8,128)S(1)}, f32[8,16,128]{2,0,1:T(8,128)S(1)}, u32[]{:S(2)}, u32[]{:S(2)}) collective-permute-start(f32[8,16,128]{2,0,1:T(8,128)S(1)} %bitcast.346), channel_id=1, source_target_pairs={{0,24},{8,32},{16,40},{24,48},{32,56},{40,64},{48,72},{56,80},{64,... | collective-permute-start | bytes 196616 | tf_op jit(solution)/shard_map/ppermute | solution.py:14
  19.3 26.7 %collective-permute-start.16 = (f32[8,16,128]{2,0,1:T(8,128)S(1)}, f32[8,16,128]{2,0,1:T(8,128)S(1)}, u32[]{:S(2)}, u32[]{:S(2)}) collective-permute-start(f32[8,16,128]{2,0,1:T(8,128)S(1)} %bitcast.345), channel_id=1, source_target_pairs={{0,16},{8,24},{16,32},{24,40},{32,48},{40,56},{48,64},{56,72},{64,... | collective-permute-start | bytes 196616 | tf_op jit(solution)/shard_map/ppermute | solution.py:14
  25.8 23.0 %collective-permute-start.15 = (f32[8,16,128]{2,0,1:T(8,128)}, f32[8,16,128]{2,0,1:T(8,128)S(1)}, u32[]{:S(2)}, u32[]{:S(2)}) collective-permute-start(f32[8,16,128]{2,0,1:T(8,128)} %fusion.149), channel_id=1, source_target_pairs={{0,8},{8,16},{16,24},{24,32},{32,40},{40,48},{48,56},{56,64},{64,7... | collective-permute-start | bytes 196616 | tf_op jit(solution)/shard_map/ppermute | solution.py:14
  31.2 19.6 %collective-permute-start.14 = (f32[8,16,128]{2,0,1:T(8,128)}, f32[8,16,128]{2,0,1:T(8,128)S(1)}, u32[]{:S(2)}, u32[]{:S(2)}) collective-permute-start(f32[8,16,128]{2,0,1:T(8,128)} %fusion.150), channel_id=1, source_target_pairs={{0,504},{8,0},{16,8},{24,16},{32,24},{40,32},{48,40},{56,48},{64,5... | collective-permute-start | bytes 196616 | tf_op jit(solution)/shard_map/ppermute | solution.py:14
  37.3 15.5 %collective-permute-start.13 = (f32[8,16,128]{2,0,1:T(8,128)S(1)}, f32[8,16,128]{2,0,1:T(8,128)S(1)}, u32[]{:S(2)}, u32[]{:S(2)}) collective-permute-start(f32[8,16,128]{2,0,1:T(8,128)S(1)} %bitcast.347), channel_id=1, source_target_pairs={{0,496},{8,504},{16,0},{24,8},{32,16},{40,24},{48,32},{56,40},{64,... | collective-permute-start | bytes 196616 | tf_op jit(solution)/shard_map/ppermute | solution.py:14
  42.8 15.3 %collective-permute-start.12 = (f32[8,16,128]{2,0,1:T(8,128)S(1)}, f32[8,16,128]{2,0,1:T(8,128)S(1)}, u32[]{:S(2)}, u32[]{:S(2)}) collective-permute-start(f32[8,16,128]{2,0,1:T(8,128)S(1)} %bitcast.348), channel_id=1, source_target_pairs={{0,488},{8,496},{16,504},{24,0},{32,8},{40,16},{48,24},{56,32},{64... | collective-permute-start | bytes 196616 | tf_op jit(solution)/shard_map/ppermute | solution.py:14
  46.0 57.2 %collective-permute-start = (bf16[64,2048]{1,0:T(8,128)(2,1)S(1)}, bf16[64,2048]{1,0:T(8,128)(2,1)S(1)}, u32[]{:S(2)}, u32[]{:S(2)}) collective-permute-start(bf16[64,2048]{1,0:T(8,128)(2,1)S(1)} %convolution_convert_fusion), channel_id=1, source_target_pairs={{0,8},{8,16},{16,24},{24,32},{32,40},{40,48},{48,56},{56,64},{64,7... | collective-permute-start | bytes 786440 | tf_op jit(solution)/shard_map/ppermute | solution.py:14
  48.8 56.3 %collective-permute-start.2 = (bf16[64,2048]{1,0:T(8,128)(2,1)S(1)}, bf16[64,2048]{1,0:T(8,128)(2,1)S(1)}, u32[]{:S(2)}, u32[]{:S(2)}) collective-permute-start(bf16[64,2048]{1,0:T(8,128)(2,1)S(1)} %convolution_convert_fusion), channel_id=1, source_target_pairs={{0,24},{8,32},{16,40},{24,48},{32,56},{40,64},{48,72},{56,80},{64,... | collective-permute-start | bytes 786440 | tf_op jit(solution)/shard_map/ppermute | solution.py:14
  50.8 54.4 %collective-permute-start.3 = (bf16[64,2048]{1,0:T(8,128)(2,1)S(1)}, bf16[64,2048]{1,0:T(8,128)(2,1)S(1)}, u32[]{:S(2)}, u32[]{:S(2)}) collective-permute-start(bf16[64,2048]{1,0:T(8,128)(2,1)S(1)} %convolution_convert_fusion), channel_id=1, source_target_pairs={{0,16},{8,24},{16,32},{24,40},{32,48},{40,56},{48,64},{56,72},{64,... | collective-permute-start | bytes 786440 | tf_op jit(solution)/shard_map/ppermute | solution.py:14
  52.7 52.5 %collective-permute-start.1 = (bf16[64,2048]{1,0:T(8,128)(2,1)S(1)}, bf16[64,2048]{1,0:T(8,128)(2,1)S(1)}, u32[]{:S(2)}, u32[]{:S(2)}) collective-permute-start(bf16[64,2048]{1,0:T(8,128)(2,1)S(1)} %convolution_convert_fusion), channel_id=1, source_target_pairs={{0,504},{8,0},{16,8},{24,16},{32,24},{40,32},{48,40},{56,48},{64,5... | collective-permute-start | bytes 786440 | tf_op jit(solution)/shard_map/ppermute | solution.py:14
  58.1 47.3 %collective-permute-start.4 = (bf16[64,2048]{1,0:T(8,128)(2,1)S(1)}, bf16[64,2048]{1,0:T(8,128)(2,1)S(1)}, u32[]{:S(2)}, u32[]{:S(2)}) collective-permute-start(bf16[64,2048]{1,0:T(8,128)(2,1)S(1)} %convolution_convert_fusion), channel_id=1, source_target_pairs={{0,496},{8,504},{16,0},{24,8},{32,16},{40,24},{48,32},{56,40},{64,... | collective-permute-start | bytes 786440 | tf_op jit(solution)/shard_map/ppermute | solution.py:14
  103.1 10.0 %collective-permute-start.5 = (bf16[64,2048]{1,0:T(8,128)(2,1)S(1)}, bf16[64,2048]{1,0:T(8,128)(2,1)S(1)}, u32[]{:S(2)}, u32[]{:S(2)}) collective-permute-start(bf16[64,2048]{1,0:T(8,128)(2,1)S(1)} %convolution_convert_fusion), channel_id=1, source_target_pairs={{0,488},{8,496},{16,504},{24,0},{32,8},{40,16},{48,24},{56,32},{64... | collective-permute-start | bytes 786440 | tf_op jit(solution)/shard_map/ppermute | solution.py:14
  124.9 26.5 %collective-permute-start.23 = (f32[64,16,128]{2,0,1:T(8,128)S(1)}, f32[64,16,128]{2,0,1:T(8,128)}, u32[]{:S(2)}, u32[]{:S(2)}) collective-permute-start(f32[64,16,128]{2,0,1:T(8,128)S(1)} %bitcast.333), channel_id=1, source_target_pairs={{0,24},{8,32},{16,40},{24,48},{32,56},{40,64},{48,72},{56,80},{64,... | collective-permute-start | bytes 1572872 | tf_op jit(solution)/shard_map/ppermute | solution.py:14
  128.5 32.7 %collective-permute-start.22 = (f32[64,16,128]{2,0,1:T(8,128)}, f32[64,16,128]{2,0,1:T(8,128)}, u32[]{:S(2)}, u32[]{:S(2)}) collective-permute-start(f32[64,16,128]{2,0,1:T(8,128)} %bitcast.314), channel_id=1, source_target_pairs={{0,16},{8,24},{16,32},{24,40},{32,48},{40,56},{48,64},{56,72},{64,... | collective-permute-start | bytes 1572872 | tf_op jit(solution)/shard_map/ppermute | solution.py:14
  132.5 22.2 %copy-start.4 = (f32[64,16,128]{2,0,1:T(8,128)}, f32[64,16,128]{2,0,1:T(8,128)S(1)}, u32[]{:S(2)}) copy-start(f32[64,16,128]{2,0,1:T(8,128)S(1)} %convolution_bitcast_fusion) | copy-start | bytes 1572868
  133.1 30.6 %collective-permute-start.21 = (f32[64,16,128]{2,0,1:T(8,128)}, f32[64,16,128]{2,0,1:T(8,128)}, u32[]{:S(2)}, u32[]{:S(2)}) collective-permute-start(f32[64,16,128]{2,0,1:T(8,128)} %fusion.104), channel_id=1, source_target_pairs={{0,8},{8,16},{16,24},{24,32},{32,40},{40,48},{48,56},{56,64},{64,7... | collective-permute-start | bytes 1572872 | tf_op jit(solution)/shard_map/ppermute | solution.py:14
  135.9 7.5 %copy-start.15 = (pred[12]{0:T(512)(128)(4,1)S(1)}, pred[12]{0:T(512)(128)(4,1)}, u32[]{:S(2)}) copy-start(pred[12]{0:T(512)(128)(4,1)} %copy-done.14) | copy-start | bytes 40
  136.9 8.1 %copy-start.13 = (pred[12]{0:T(512)(128)(4,1)S(1)}, pred[12]{0:T(512)(128)(4,1)}, u32[]{:S(2)}) copy-start(pred[12]{0:T(512)(128)(4,1)} %copy-done.12) | copy-start | bytes 40
  137.2 8.6 %copy-start.5 = (f32[64,16,128]{2,0,1:T(8,128)}, f32[64,16,128]{2,0,1:T(8,128)S(1)}, u32[]{:S(2)}) copy-start(f32[64,16,128]{2,0,1:T(8,128)S(1)} %convolution_bitcast_fusion.1) | copy-start | bytes 1572868
  137.8 25.9 %collective-permute-start.20 = (f32[64,16,128]{2,0,1:T(8,128)}, f32[64,16,128]{2,0,1:T(8,128)}, u32[]{:S(2)}, u32[]{:S(2)}) collective-permute-start(f32[64,16,128]{2,0,1:T(8,128)} %fusion.105), channel_id=1, source_target_pairs={{0,504},{8,0},{16,8},{24,16},{32,24},{40,32},{48,40},{56,48},{64,5... | collective-permute-start | bytes 1572872 | tf_op jit(solution)/shard_map/ppermute | solution.py:14
  145.7 9.0 %copy-start.3 = (bf16[64,2048]{1,0:T(8,128)(2,1)S(1)}, bf16[64,2048]{1,0:T(8,128)(2,1)}, u32[]{:S(2)}) copy-start(bf16[64,2048]{1,0:T(8,128)(2,1)} %fusion.45) | copy-start | bytes 786436
  145.8 17.9 %collective-permute-start.19 = (f32[64,16,128]{2,0,1:T(8,128)}, f32[64,16,128]{2,0,1:T(8,128)}, u32[]{:S(2)}, u32[]{:S(2)}) collective-permute-start(f32[64,16,128]{2,0,1:T(8,128)} %bitcast.315), channel_id=1, source_target_pairs={{0,496},{8,504},{16,0},{24,8},{32,16},{40,24},{48,32},{56,40},{64,... | collective-permute-start | bytes 1572872 | tf_op jit(solution)/shard_map/ppermute | solution.py:14
  151.4 27.1 %collective-permute-start.18 = (f32[64,16,128]{2,0,1:T(8,128)}, f32[64,16,128]{2,0,1:T(8,128)}, u32[]{:S(2)}, u32[]{:S(2)}) collective-permute-start(f32[64,16,128]{2,0,1:T(8,128)} %bitcast.316), channel_id=1, source_target_pairs={{0,488},{8,496},{16,504},{24,0},{32,8},{40,16},{48,24},{56,32},{64... | collective-permute-start | bytes 1572872 | tf_op jit(solution)/shard_map/ppermute | solution.py:14
  154.7 23.8 %slice-start.1 = ((f32[64,16,128]{2,0,1:T(8,128)}), f32[64,15,128]{2,0,1:T(8,128)S(1)}, s32[]{:S(2)}) async-start(f32[64,16,128]{2,0,1:T(8,128)} %copy-done.5), calls=%async_computation.2 | async-start | bytes 983040 | tf_op jit(solution)/shard_map/slice | solution.py:103
  154.7 23.8 %slice-start = ((f32[64,16,128]{2,0,1:T(8,128)}), f32[64,15,128]{2,0,1:T(8,128)S(1)}, s32[]{:S(2)}) async-start(f32[64,16,128]{2,0,1:T(8,128)} %copy-done.4), calls=%async_computation.1 | async-start | bytes 983040 | tf_op jit(solution)/shard_map/slice | solution.py:104
  390.5 24.0 %copy-start.25 = (pred[12]{0:T(512)(128)(4,1)S(1)}, pred[12]{0:T(512)(128)(4,1)}, u32[]{:S(2)}) copy-start(pred[12]{0:T(512)(128)(4,1)} %copy-done.24) | copy-start | bytes 40
  390.5 24.3 %copy-start.28 = (pred[12]{0:T(512)(128)(4,1)S(1)}, pred[12]{0:T(512)(128)(4,1)}, u32[]{:S(2)}) copy-start(pred[12]{0:T(512)(128)(4,1)} %copy-done.27) | copy-start | bytes 40
  392.9 18.8 %collective-permute-start.6 = (bf16[8,2048]{1,0:T(8,128)(2,1)S(1)}, bf16[8,2048]{1,0:T(8,128)(2,1)S(1)}, u32[]{:S(2)}, u32[]{:S(2)}) collective-permute-start(bf16[8,2048]{1,0:T(8,128)(2,1)S(1)} %convolution_convert_fusion.1), channel_id=1, source_target_pairs={{0,8},{8,16},{16,24},{24,32},{32,40},{40,48},{48,56},{56,64},{64,7... | collective-permute-start | bytes 98312 | tf_op jit(solution)/shard_map/ppermute | solution.py:14
  394.9 13.3 %collective-permute-start.8 = (bf16[8,2048]{1,0:T(8,128)(2,1)S(1)}, bf16[8,2048]{1,0:T(8,128)(2,1)S(1)}, u32[]{:S(2)}, u32[]{:S(2)}) collective-permute-start(bf16[8,2048]{1,0:T(8,128)(2,1)S(1)} %convolution_convert_fusion.1), channel_id=1, source_target_pairs={{0,24},{8,32},{16,40},{24,48},{32,56},{40,64},{48,72},{56,80},{64,... | collective-permute-start | bytes 98312 | tf_op jit(solution)/shard_map/ppermute | solution.py:14
  396.8 14.9 %collective-permute-start.9 = (bf16[8,2048]{1,0:T(8,128)(2,1)S(1)}, bf16[8,2048]{1,0:T(8,128)(2,1)S(1)}, u32[]{:S(2)}, u32[]{:S(2)}) collective-permute-start(bf16[8,2048]{1,0:T(8,128)(2,1)S(1)} %convolution_convert_fusion.1), channel_id=1, source_target_pairs={{0,16},{8,24},{16,32},{24,40},{32,48},{40,56},{48,64},{56,72},{64,... | collective-permute-start | bytes 98312 | tf_op jit(solution)/shard_map/ppermute | solution.py:14
  398.7 13.0 %collective-permute-start.7 = (bf16[8,2048]{1,0:T(8,128)(2,1)S(1)}, bf16[8,2048]{1,0:T(8,128)(2,1)S(1)}, u32[]{:S(2)}, u32[]{:S(2)}) collective-permute-start(bf16[8,2048]{1,0:T(8,128)(2,1)S(1)} %convolution_convert_fusion.1), channel_id=1, source_target_pairs={{0,504},{8,0},{16,8},{24,16},{32,24},{40,32},{48,40},{56,48},{64,5... | collective-permute-start | bytes 98312 | tf_op jit(solution)/shard_map/ppermute | solution.py:14
  404.5 7.3 %collective-permute-start.10 = (bf16[8,2048]{1,0:T(8,128)(2,1)S(1)}, bf16[8,2048]{1,0:T(8,128)(2,1)S(1)}, u32[]{:S(2)}, u32[]{:S(2)}) collective-permute-start(bf16[8,2048]{1,0:T(8,128)(2,1)S(1)} %convolution_convert_fusion.1), channel_id=1, source_target_pairs={{0,496},{8,504},{16,0},{24,8},{32,16},{40,24},{48,32},{56,40},{64,... | collective-permute-start | bytes 98312 | tf_op jit(solution)/shard_map/ppermute | solution.py:14
  408.2 5.8 %collective-permute-start.11 = (bf16[8,2048]{1,0:T(8,128)(2,1)S(1)}, bf16[8,2048]{1,0:T(8,128)(2,1)S(1)}, u32[]{:S(2)}, u32[]{:S(2)}) collective-permute-start(bf16[8,2048]{1,0:T(8,128)(2,1)S(1)} %convolution_convert_fusion.1), channel_id=1, source_target_pairs={{0,488},{8,496},{16,504},{24,0},{32,8},{40,16},{48,24},{56,32},{64... | collective-permute-start | bytes 98312 | tf_op jit(solution)/shard_map/ppermute | solution.py:14
  (8 other events, 25.6 us)
Sparse Core Ops, SparseCore 0:
  121.1 77.6 all-gather.1
where the time goes:
time: 425 us; the launch traced here: 423 us
  blocking collectives  251 us (59%)
  starting transfers between devices  79.6 us (19%)
  waiting for transfers between devices  31.7 us (7%)
  matrix products  21.6 us (5%)
  local copies, waits for them, and re-layouts  18 us (4%)
  between operations  15.3 us (4%)
  other arithmetic  6.68 us (2%)
    psum x1, blocking collectives, local(): first_grad, second_grad = lax.psum((first_part, second_part), 'row')  210 us
    ppermute x24, starting transfers between devices, passed_along(): lax.ppermute(x, axis, [(i, (i + by) % devices) for i in range(devices)])  79.6 us
    all_gather x1, blocking collectives, local(): shard_piece = lax.all_gather(class_back, 'col', axis=0, tiled=True)  41 us
    ppermute x24, waiting for transfers between devices, passed_along(): lax.ppermute(x, axis, [(i, (i + by) % devices) for i in range(devices)])  31.7 us
  transfers between devices with their start and end apart: 25, of which 5 were waited for; matrix products, arithmetic and copies ran while one was open for 6% of the time, Pallas kernels for 0%

commit v1 on v0

--- a/solution.py
+++ b/solution.py
@@ -157,7 +157,9 @@
     class_back = aggregate_back(
         score_grad, band_blocks, long_blocks, row_ids, long_sources, long_counts
     ).astype(jnp.bfloat16)
-    shard_piece = lax.all_gather(class_back, "col", axis=0, tiled=True)
+    shard_piece = jnp.concatenate(
+        lax.all_to_all(jnp.stack([class_back] * lax.axis_size("col")), "col", 0, 0), axis=0
+    )
     hidden_back = jnp.einsum("hc,cn->hn", my_rows, shard_piece, preferred_element_type=jnp.float32)
     block_grad = jnp.einsum(
         "hn,cn->hc", hidden_act, shard_piece, preferred_element_type=jnp.float32

time: 425 us -> 396 us (0.932)
  the two profiles are of different devices: /device:TPU:2 before, /device:TPU:1 now
where the time goes in v1:
time: 396 us; the launch traced here: 395 us
  blocking collectives  203 us (51%)
  starting transfers between devices  98.7 us (25%)
  local copies, waits for them, and re-layouts  24.5 us (6%)
  matrix products  22.8 us (6%)
  waiting for transfers between devices  22.2 us (6%)
  between operations  15.2 us (4%)
  other arithmetic  7.74 us (2%)
    psum x1, blocking collectives, local(): first_grad, second_grad = lax.psum((first_part, second_part), 'row')  203 us
    ppermute x24, starting transfers between devices, passed_along(): lax.ppermute(x, axis, [(i, (i + by) % devices) for i in range(devices)])  92.3 us
    ppermute x24, waiting for transfers between devices, passed_along(): lax.ppermute(x, axis, [(i, (i + by) % devices) for i in range(devices)])  22.1 us
    unnamed x84, local copies, waits for them, and re-layouts  8.34 us
  transfers between devices with their start and end apart: 26, of which 5 were waited for; matrix products, arithmetic and copies ran while one was open for 12% of the time, Pallas kernels for 0%

profile of v1, /device:TPU:1, one launch (start us, length us, event | category | flops | bytes accessed | tf_op | source)
XLA Modules:
  0.0 394.5 jit_solution(14340643697248574760)
XLA Ops:
  9.2 6.3 %collective-permute-start.2 = (bf16[64,2048]{1,0:T(8,128)(2,1)S(1)}, bf16[64,2048]{1,0:T(8,128)(2,1)S(1)}, u32[]{:S(2)}, u32[]{:S(2)}) collective-permute-start(bf16[64,2048]{1,0:T(8,128)(2,1)S(1)} %convolution_convert_fusion), channel_id=1, source_target_pairs={{0,24},{8,32},{16,40},{24,48},{32,56},{40,64},{48,72},{56,80},{64,... | collective-permute-start | bytes 786440 | tf_op jit(solution)/shard_map/ppermute | solution.py:14
  15.5 1.2 dynamic_slice.22
  17.6 1.2 iota_compare_fusion.2
  19.5 1.2 fusion.192
  20.7 1.9 compare_and_fusion.4
  22.6 1.3 gather_fusion.2
  23.9 1.3 convolution_multiply_fusion.3
  25.7 4.4 %collective-permute-start.14 = (f32[8,16,128]{2,0,1:T(8,128)S(1)}, f32[8,16,128]{2,0,1:T(8,128)S(1)}, u32[]{:S(2)}, u32[]{:S(2)}) collective-permute-start(f32[8,16,128]{2,0,1:T(8,128)S(1)} %fusion.155), channel_id=1, source_target_pairs={{0,504},{8,0},{16,8},{24,16},{32,24},{40,32},{48,40},{56,48},{64,5... | collective-permute-start | bytes 196616 | tf_op jit(solution)/shard_map/ppermute | solution.py:14
  30.6 1.9 collective-permute-start.15
  32.7 9.8 %collective-permute-start.13 = (f32[8,16,128]{2,0,1:T(8,128)S(1)}, f32[8,16,128]{2,0,1:T(8,128)}, u32[]{:S(2)}, u32[]{:S(2)}) collective-permute-start(f32[8,16,128]{2,0,1:T(8,128)S(1)} %bitcast.352), channel_id=1, source_target_pairs={{0,496},{8,504},{16,0},{24,8},{32,16},{40,24},{48,32},{56,40},{64,... | collective-permute-start | bytes 196616 | tf_op jit(solution)/shard_map/ppermute | solution.py:14
  42.9 1.9 collective-permute-start.16
  46.5 1.9 collective-permute-start.17
  48.5 5.8 %collective-permute-start.12 = (f32[8,16,128]{2,0,1:T(8,128)}, f32[8,16,128]{2,0,1:T(8,128)}, u32[]{:S(2)}, u32[]{:S(2)}) collective-permute-start(f32[8,16,128]{2,0,1:T(8,128)} %bitcast.331), channel_id=1, source_target_pairs={{0,488},{8,496},{16,504},{24,0},{32,8},{40,16},{48,24},{56,32},{64... | collective-permute-start | bytes 196616 | tf_op jit(solution)/shard_map/ppermute | solution.py:14
  55.1 1.9 collective-permute-start.3
  57.0 3.1 collective-permute-start
  60.1 2.3 collective-permute-start.1
  62.5 5.4 %collective-permute-start.4 = (bf16[64,2048]{1,0:T(8,128)(2,1)S(1)}, bf16[64,2048]{1,0:T(8,128)(2,1)}, u32[]{:S(2)}, u32[]{:S(2)}) collective-permute-start(bf16[64,2048]{1,0:T(8,128)(2,1)S(1)} %convolution_convert_fusion), channel_id=1, source_target_pairs={{0,496},{8,504},{16,0},{24,8},{32,16},{40,24},{48,32},{56,40},{64,... | collective-permute-start | bytes 786440 | tf_op jit(solution)/shard_map/ppermute | solution.py:14
  67.8 1.2 pad_clamp_fusion.1
  69.1 1.9 collective-permute-start.5
  71.0 1.3 fusion.26
  73.0 6.4 %all-to-all-start = ((bf16[8,8,2048]{2,1,0:T(8,128)(2,1)}), bf16[8,8,2048]{2,1,0:T(8,128)(2,1)}, u32[]{:S(2)}, u32[]{:S(2)}) async-start(bf16[8,8,2048]{2,1,0:T(8,128)(2,1)} %stack.8), calls=%async_computation | async-start | bytes 524288 | tf_op jit(solution)/shard_map/all_to_all | solution.py:161
  85.4 1.2 copy-done.7
  86.6 2.1 gather_fusion
  89.8 1.4 fusion.11
  92.2 1.4 fusion.14
  94.4 1.7 gather_fusion.3
  97.6 3.8 collective-permute-start.20
  105.4 1.9 collective-permute-start.21
  108.3 7.5 %collective-permute-start.19 = (f32[64,16,128]{2,0,1:T(8,128)}, f32[64,16,128]{2,0,1:T(8,128)}, u32[]{:S(2)}, u32[]{:S(2)}) collective-permute-start(f32[64,16,128]{2,0,1:T(8,128)} %bitcast.325), channel_id=1, source_target_pairs={{0,496},{8,504},{16,0},{24,8},{32,16},{40,24},{48,32},{56,40},{64,... | collective-permute-start | bytes 1572872 | tf_op jit(solution)/shard_map/ppermute | solution.py:14
  116.8 1.9 collective-permute-start.22
  121.1 6.1 %collective-permute-start.18 = (f32[64,16,128]{2,0,1:T(8,128)}, f32[64,16,128]{2,0,1:T(8,128)}, u32[]{:S(2)}, u32[]{:S(2)}) collective-permute-start(f32[64,16,128]{2,0,1:T(8,128)} %bitcast.326), channel_id=1, source_target_pairs={{0,488},{8,496},{16,504},{24,0},{32,8},{40,16},{48,24},{56,32},{64... | collective-permute-start | bytes 1572872 | tf_op jit(solution)/shard_map/ppermute | solution.py:14
  128.2 1.9 collective-permute-start.23
  130.1 1.0 copy-done.6
  131.2 1.3 fusion.74
  132.5 1.9 collective-permute-done.22
  134.4 10.3 %collective-permute-done.18 = f32[64,16,128]{2,0,1:T(8,128)} collective-permute-done((f32[64,16,128]{2,0,1:T(8,128)}, f32[64,16,128]{2,0,1:T(8,128)}, u32[]{:S(2)}, u32[]{:S(2)}) %collective-permute-start.18) | collective-permute-done | bytes 524320 | tf_op jit(solution)/shard_map/ppermute | solution.py:14
  144.7 7.5 %collective-permute-done.23 = f32[64,16,128]{2,0,1:T(8,128)} collective-permute-done((f32[64,16,128]{2,0,1:T(8,128)}, f32[64,16,128]{2,0,1:T(8,128)}, u32[]{:S(2)}, u32[]{:S(2)}) %collective-permute-start.23) | collective-permute-done | bytes 524320 | tf_op jit(solution)/shard_map/ppermute | solution.py:14
  152.3 2.2 fusion.13
  154.8 203.4 %all-reduce.4 = (f32[128,64]{0,1:T(8,128)}, f32[64,64]{1,0:T(8,128)}) all-reduce(f32[128,64]{0,1:T(8,128)S(1)} %convolution_bitcast_fusion.6, f32[64,64]{1,0:T(8,128)S(1)} %fusion.74), channel_id=1, replica_groups=mesh['row'=64,'col'=8] {'row'}, use_global_device_ids=true, to_apply=%region_0.1 | all-reduce | flops 12288 | bytes 98304 | tf_op jit(solution)/shard_map/psum | solution.py:177
  358.3 2.0 convolution_convert_fusion.1
  360.3 1.9 collective-permute-start.8
  362.2 1.9 collective-permute-start.9
  364.1 3.6 collective-permute-start.6
  367.7 4.7 %collective-permute-start.7 = (bf16[8,2048]{1,0:T(8,128)(2,1)S(1)}, bf16[8,2048]{1,0:T(8,128)(2,1)S(1)}, u32[]{:S(2)}, u32[]{:S(2)}) collective-permute-start(bf16[8,2048]{1,0:T(8,128)(2,1)S(1)} %convolution_convert_fusion.1), channel_id=1, source_target_pairs={{0,504},{8,0},{16,8},{24,16},{32,24},{40,32},{48,40},{56,48},{64,5... | collective-permute-start | bytes 98312 | tf_op jit(solution)/shard_map/ppermute | solution.py:14
  372.4 5.8 %collective-permute-start.10 = (bf16[8,2048]{1,0:T(8,128)(2,1)S(1)}, bf16[8,2048]{1,0:T(8,128)(2,1)S(1)}, u32[]{:S(2)}, u32[]{:S(2)}) collective-permute-start(bf16[8,2048]{1,0:T(8,128)(2,1)S(1)} %convolution_convert_fusion.1), channel_id=1, source_target_pairs={{0,496},{8,504},{16,0},{24,8},{32,16},{40,24},{48,32},{56,40},{64,... | collective-permute-start | bytes 98312 | tf_op jit(solution)/shard_map/ppermute | solution.py:14
  378.5 4.7 %collective-permute-start.11 = (bf16[8,2048]{1,0:T(8,128)(2,1)S(1)}, bf16[8,2048]{1,0:T(8,128)(2,1)S(1)}, u32[]{:S(2)}, u32[]{:S(2)}) collective-permute-start(bf16[8,2048]{1,0:T(8,128)(2,1)S(1)} %convolution_convert_fusion.1), channel_id=1, source_target_pairs={{0,488},{8,496},{16,504},{24,0},{32,8},{40,16},{48,24},{56,32},{64... | collective-permute-start | bytes 98312 | tf_op jit(solution)/shard_map/ppermute | solution.py:14
  383.4 1.6 collective-permute-done.11
  386.6 1.0 fusion.28
  (171 shorter events, 29.9 us)
Async XLA Ops:
  7.2 18.3 %copy-start.8 = (bf16[8,2048]{1,0:T(8,128)(2,1)S(1)}, bf16[8,2048]{1,0:T(8,128)(2,1)}, u32[]{:S(2)}) copy-start(bf16[8,2048]{1,0:T(8,128)(2,1)} %param.20) | copy-start | bytes 98308
  7.2 18.2 %copy-start.1 = (bf16[16,3,128,128]{3,2,1,0:T(8,128)(2,1)S(1)}, bf16[16,3,128,128]{3,2,1,0:T(8,128)(2,1)}, u32[]{:S(2)}) copy-start(bf16[16,3,128,128]{3,2,1,0:T(8,128)(2,1)} %param.21) | copy-start | bytes 4718596
  9.2 59.9 %collective-permute-start.2 = (bf16[64,2048]{1,0:T(8,128)(2,1)S(1)}, bf16[64,2048]{1,0:T(8,128)(2,1)S(1)}, u32[]{:S(2)}, u32[]{:S(2)}) collective-permute-start(bf16[64,2048]{1,0:T(8,128)(2,1)S(1)} %convolution_convert_fusion), channel_id=1, source_target_pairs={{0,24},{8,32},{16,40},{24,48},{32,56},{40,64},{48,72},{56,80},{64,... | collective-permute-start | bytes 786440 | tf_op jit(solution)/shard_map/ppermute | solution.py:14
  19.5 25.6 %copy-start.13 = (pred[12]{0:T(512)(128)(4,1)}, pred[12]{0:T(512)(128)(4,1)S(1)}, u32[]{:S(2)}) copy-start(pred[12]{0:T(512)(128)(4,1)S(1)} %get-tuple-element.53) | copy-start | bytes 40
  20.7 4.5 %copy-start.12 = (s32[1024]{0:T(1024)}, s32[1024]{0:T(1024)S(1)}, u32[]{:S(2)}) copy-start(s32[1024]{0:T(1024)S(1)} %pad_clamp_fusion) | copy-start | bytes 12292
  22.6 20.2 %copy-start.17 = (pred[12]{0:T(512)(128)(4,1)}, pred[12]{0:T(512)(128)(4,1)S(1)}, u32[]{:S(2)}) copy-start(pred[12]{0:T(512)(128)(4,1)S(1)} %get-tuple-element.74) | copy-start | bytes 40
  22.6 20.2 %copy-start.19 = (pred[12]{0:T(512)(128)(4,1)}, pred[12]{0:T(512)(128)(4,1)S(1)}, u32[]{:S(2)}) copy-start(pred[12]{0:T(512)(128)(4,1)S(1)} %get-tuple-element.70) | copy-start | bytes 40
  22.6 20.2 %copy-start.21 = (pred[12]{0:T(512)(128)(4,1)}, pred[12]{0:T(512)(128)(4,1)S(1)}, u32[]{:S(2)}) copy-start(pred[12]{0:T(512)(128)(4,1)S(1)} %get-tuple-element.72) | copy-start | bytes 40
  22.6 20.2 %copy-start.23 = (pred[12]{0:T(512)(128)(4,1)}, pred[12]{0:T(512)(128)(4,1)S(1)}, u32[]{:S(2)}) copy-start(pred[12]{0:T(512)(128)(4,1)S(1)} %get-tuple-element.71) | copy-start | bytes 40
  22.6 20.2 %copy-start.27 = (pred[12]{0:T(512)(128)(4,1)}, pred[12]{0:T(512)(128)(4,1)S(1)}, u32[]{:S(2)}) copy-start(pred[12]{0:T(512)(128)(4,1)S(1)} %get-tuple-element.77) | copy-start | bytes 40
  22.6 22.3 %copy-start.15 = (pred[12]{0:T(512)(128)(4,1)}, pred[12]{0:T(512)(128)(4,1)S(1)}, u32[]{:S(2)}) copy-start(pred[12]{0:T(512)(128)(4,1)S(1)} %get-tuple-element.73) | copy-start | bytes 40
  25.7 20.8 %collective-permute-start.14 = (f32[8,16,128]{2,0,1:T(8,128)S(1)}, f32[8,16,128]{2,0,1:T(8,128)S(1)}, u32[]{:S(2)}, u32[]{:S(2)}) collective-permute-start(f32[8,16,128]{2,0,1:T(8,128)S(1)} %fusion.155), channel_id=1, source_target_pairs={{0,504},{8,0},{16,8},{24,16},{32,24},{40,32},{48,40},{56,48},{64,5... | collective-permute-start | bytes 196616 | tf_op jit(solution)/shard_map/ppermute | solution.py:14
  30.6 17.8 %collective-permute-start.15 = (f32[8,16,128]{2,0,1:T(8,128)S(1)}, f32[8,16,128]{2,0,1:T(8,128)S(1)}, u32[]{:S(2)}, u32[]{:S(2)}) collective-permute-start(f32[8,16,128]{2,0,1:T(8,128)S(1)} %fusion.154), channel_id=1, source_target_pairs={{0,8},{8,16},{16,24},{24,32},{32,40},{40,48},{48,56},{56,64},{64,7... | collective-permute-start | bytes 196616 | tf_op jit(solution)/shard_map/ppermute | solution.py:14
  32.7 22.3 %collective-permute-start.13 = (f32[8,16,128]{2,0,1:T(8,128)S(1)}, f32[8,16,128]{2,0,1:T(8,128)}, u32[]{:S(2)}, u32[]{:S(2)}) collective-permute-start(f32[8,16,128]{2,0,1:T(8,128)S(1)} %bitcast.352), channel_id=1, source_target_pairs={{0,496},{8,504},{16,0},{24,8},{32,16},{40,24},{48,32},{56,40},{64,... | collective-permute-start | bytes 196616 | tf_op jit(solution)/shard_map/ppermute | solution.py:14
  42.9 14.2 %collective-permute-start.16 = (f32[8,16,128]{2,0,1:T(8,128)S(1)}, f32[8,16,128]{2,0,1:T(8,128)}, u32[]{:S(2)}, u32[]{:S(2)}) collective-permute-start(f32[8,16,128]{2,0,1:T(8,128)S(1)} %bitcast.351), channel_id=1, source_target_pairs={{0,16},{8,24},{16,32},{24,40},{32,48},{40,56},{48,64},{56,72},{64,... | collective-permute-start | bytes 196616 | tf_op jit(solution)/shard_map/ppermute | solution.py:14
  46.5 13.6 %collective-permute-start.17 = (f32[8,16,128]{2,0,1:T(8,128)}, f32[8,16,128]{2,0,1:T(8,128)}, u32[]{:S(2)}, u32[]{:S(2)}) collective-permute-start(f32[8,16,128]{2,0,1:T(8,128)} %bitcast.328), channel_id=1, source_target_pairs={{0,24},{8,32},{16,40},{24,48},{32,56},{40,64},{48,72},{56,80},{64,... | collective-permute-start | bytes 196616 | tf_op jit(solution)/shard_map/ppermute | solution.py:14
  48.5 6.6 %copy-start.10 = (f32[8,16,128]{2,0,1:T(8,128)}, f32[8,16,128]{2,0,1:T(8,128)S(1)}, u32[]{:S(2)}) copy-start(f32[8,16,128]{2,0,1:T(8,128)S(1)} %collective-permute-done.15) | copy-start | bytes 196612
  48.5 14.0 %collective-permute-start.12 = (f32[8,16,128]{2,0,1:T(8,128)}, f32[8,16,128]{2,0,1:T(8,128)}, u32[]{:S(2)}, u32[]{:S(2)}) collective-permute-start(f32[8,16,128]{2,0,1:T(8,128)} %bitcast.331), channel_id=1, source_target_pairs={{0,488},{8,496},{16,504},{24,0},{32,8},{40,16},{48,24},{56,32},{64... | collective-permute-start | bytes 196616 | tf_op jit(solution)/shard_map/ppermute | solution.py:14
  55.1 24.3 %collective-permute-start.3 = (bf16[64,2048]{1,0:T(8,128)(2,1)S(1)}, bf16[64,2048]{1,0:T(8,128)(2,1)S(1)}, u32[]{:S(2)}, u32[]{:S(2)}) collective-permute-start(bf16[64,2048]{1,0:T(8,128)(2,1)S(1)} %convolution_convert_fusion), channel_id=1, source_target_pairs={{0,16},{8,24},{16,32},{24,40},{32,48},{40,56},{48,64},{56,72},{64,... | collective-permute-start | bytes 786440 | tf_op jit(solution)/shard_map/ppermute | solution.py:14
  57.0 22.4 %collective-permute-start = (bf16[64,2048]{1,0:T(8,128)(2,1)S(1)}, bf16[64,2048]{1,0:T(8,128)(2,1)S(1)}, u32[]{:S(2)}, u32[]{:S(2)}) collective-permute-start(bf16[64,2048]{1,0:T(8,128)(2,1)S(1)} %convolution_convert_fusion), channel_id=1, source_target_pairs={{0,8},{8,16},{16,24},{24,32},{32,40},{40,48},{48,56},{56,64},{64,7... | collective-permute-start | bytes 786440 | tf_op jit(solution)/shard_map/ppermute | solution.py:14
  60.1 19.4 %collective-permute-start.1 = (bf16[64,2048]{1,0:T(8,128)(2,1)S(1)}, bf16[64,2048]{1,0:T(8,128)(2,1)}, u32[]{:S(2)}, u32[]{:S(2)}) collective-permute-start(bf16[64,2048]{1,0:T(8,128)(2,1)S(1)} %convolution_convert_fusion), channel_id=1, source_target_pairs={{0,504},{8,0},{16,8},{24,16},{32,24},{40,32},{48,40},{56,48},{64,5... | collective-permute-start | bytes 786440 | tf_op jit(solution)/shard_map/ppermute | solution.py:14
  62.5 18.1 %collective-permute-start.4 = (bf16[64,2048]{1,0:T(8,128)(2,1)S(1)}, bf16[64,2048]{1,0:T(8,128)(2,1)}, u32[]{:S(2)}, u32[]{:S(2)}) collective-permute-start(bf16[64,2048]{1,0:T(8,128)(2,1)S(1)} %convolution_convert_fusion), channel_id=1, source_target_pairs={{0,496},{8,504},{16,0},{24,8},{32,16},{40,24},{48,32},{56,40},{64,... | collective-permute-start | bytes 786440 | tf_op jit(solution)/shard_map/ppermute | solution.py:14
  69.1 13.2 %collective-permute-start.5 = (bf16[64,2048]{1,0:T(8,128)(2,1)S(1)}, bf16[64,2048]{1,0:T(8,128)(2,1)}, u32[]{:S(2)}, u32[]{:S(2)}) collective-permute-start(bf16[64,2048]{1,0:T(8,128)(2,1)S(1)} %convolution_convert_fusion), channel_id=1, source_target_pairs={{0,488},{8,496},{16,504},{24,0},{32,8},{40,16},{48,24},{56,32},{64... | collective-permute-start | bytes 786440 | tf_op jit(solution)/shard_map/ppermute | solution.py:14
  73.0 19.3 %all-to-all-start = ((bf16[8,8,2048]{2,1,0:T(8,128)(2,1)}), bf16[8,8,2048]{2,1,0:T(8,128)(2,1)}, u32[]{:S(2)}, u32[]{:S(2)}) async-start(bf16[8,8,2048]{2,1,0:T(8,128)(2,1)} %stack.8), calls=%async_computation | async-start | bytes 524288 | tf_op jit(solution)/shard_map/all_to_all | solution.py:161
  79.3 278.9 %all-gather.2.cloned.1.call-start = ((), (), s32[]{:S(2)}) async-start(), calls=%async_computation.1 | async-start | bytes 2359296 | tf_op jit(solution)/shard_map/all_gather | solution.py:150
  84.2 4.5 %copy-start.2 = (bf16[12,128,128]{2,1,0:T(8,128)(2,1)S(1)}, bf16[12,128,128]{2,1,0:T(8,128)(2,1)}, u32[]{:S(2)}) copy-start(bf16[12,128,128]{2,1,0:T(8,128)(2,1)} %param.22) | copy-start | bytes 1179652
  84.2 4.5 %copy-start.25 = (pred[12]{0:T(512)(128)(4,1)S(1)}, pred[12]{0:T(512)(128)(4,1)}, u32[]{:S(2)}) copy-start(pred[12]{0:T(512)(128)(4,1)} %get-tuple-element.75) | copy-start | bytes 40
  97.5 32.6 %copy-start.3 = (f32[64,16,128]{2,0,1:T(8,128)}, f32[64,16,128]{2,0,1:T(8,128)S(1)}, u32[]{:S(2)}) copy-start(f32[64,16,128]{2,0,1:T(8,128)S(1)} %convolution_bitcast_fusion.1) | copy-start | bytes 1572868
  97.6 5.5 %copy-start.20 = (pred[12]{0:T(512)(128)(4,1)S(1)}, pred[12]{0:T(512)(128)(4,1)}, u32[]{:S(2)}) copy-start(pred[12]{0:T(512)(128)(4,1)} %copy-done.19) | copy-start | bytes 40
  97.6 30.6 %collective-permute-start.20 = (f32[64,16,128]{2,0,1:T(8,128)S(1)}, f32[64,16,128]{2,0,1:T(8,128)}, u32[]{:S(2)}, u32[]{:S(2)}) collective-permute-start(f32[64,16,128]{2,0,1:T(8,128)S(1)} %fusion.110), channel_id=1, source_target_pairs={{0,504},{8,0},{16,8},{24,16},{32,24},{40,32},{48,40},{56,48},{64,5... | collective-permute-start | bytes 1572872 | tf_op jit(solution)/shard_map/ppermute | solution.py:14
  104.5 14.2 %copy-start.14 = (pred[12]{0:T(512)(128)(4,1)S(1)}, pred[12]{0:T(512)(128)(4,1)}, u32[]{:S(2)}) copy-start(pred[12]{0:T(512)(128)(4,1)} %copy-done.13) | copy-start | bytes 40
  104.8 14.7 %copy-start.4 = (f32[64,16,128]{2,0,1:T(8,128)}, f32[64,16,128]{2,0,1:T(8,128)S(1)}, u32[]{:S(2)}) copy-start(f32[64,16,128]{2,0,1:T(8,128)S(1)} %convolution_bitcast_fusion) | copy-start | bytes 1572868
  105.4 27.1 %collective-permute-start.21 = (f32[64,16,128]{2,0,1:T(8,128)}, f32[64,16,128]{2,0,1:T(8,128)}, u32[]{:S(2)}, u32[]{:S(2)}) collective-permute-start(f32[64,16,128]{2,0,1:T(8,128)} %fusion.109), channel_id=1, source_target_pairs={{0,8},{8,16},{16,24},{24,32},{32,40},{40,48},{48,56},{56,64},{64,7... | collective-permute-start | bytes 1572872 | tf_op jit(solution)/shard_map/ppermute | solution.py:14
  108.3 12.1 %copy-start.16 = (pred[12]{0:T(512)(128)(4,1)S(1)}, pred[12]{0:T(512)(128)(4,1)}, u32[]{:S(2)}) copy-start(pred[12]{0:T(512)(128)(4,1)} %copy-done.15) | copy-start | bytes 40
  108.3 24.2 %collective-permute-start.19 = (f32[64,16,128]{2,0,1:T(8,128)}, f32[64,16,128]{2,0,1:T(8,128)}, u32[]{:S(2)}, u32[]{:S(2)}) collective-permute-start(f32[64,16,128]{2,0,1:T(8,128)} %bitcast.325), channel_id=1, source_target_pairs={{0,496},{8,504},{16,0},{24,8},{32,16},{40,24},{48,32},{56,40},{64,... | collective-permute-start | bytes 1572872 | tf_op jit(solution)/shard_map/ppermute | solution.py:14
  116.8 17.6 %collective-permute-start.22 = (f32[64,16,128]{2,0,1:T(8,128)}, f32[64,16,128]{2,0,1:T(8,128)}, u32[]{:S(2)}, u32[]{:S(2)}) collective-permute-start(f32[64,16,128]{2,0,1:T(8,128)} %bitcast.324), channel_id=1, source_target_pairs={{0,16},{8,24},{16,32},{24,40},{32,48},{40,56},{48,64},{56,72},{64,... | collective-permute-start | bytes 1572872 | tf_op jit(solution)/shard_map/ppermute | solution.py:14
  121.1 23.6 %collective-permute-start.18 = (f32[64,16,128]{2,0,1:T(8,128)}, f32[64,16,128]{2,0,1:T(8,128)}, u32[]{:S(2)}, u32[]{:S(2)}) collective-permute-start(f32[64,16,128]{2,0,1:T(8,128)} %bitcast.326), channel_id=1, source_target_pairs={{0,488},{8,496},{16,504},{24,0},{32,8},{40,16},{48,24},{56,32},{64... | collective-permute-start | bytes 1572872 | tf_op jit(solution)/shard_map/ppermute | solution.py:14
  128.2 24.1 %collective-permute-start.23 = (f32[64,16,128]{2,0,1:T(8,128)}, f32[64,16,128]{2,0,1:T(8,128)}, u32[]{:S(2)}, u32[]{:S(2)}) collective-permute-start(f32[64,16,128]{2,0,1:T(8,128)} %bitcast.323), channel_id=1, source_target_pairs={{0,24},{8,32},{16,40},{24,48},{32,56},{40,64},{48,72},{56,80},{64,... | collective-permute-start | bytes 1572872 | tf_op jit(solution)/shard_map/ppermute | solution.py:14
  131.1 21.1 %slice-start = ((f32[64,16,128]{2,0,1:T(8,128)}), f32[64,15,128]{2,0,1:T(8,128)S(1)}, s32[]{:S(2)}) async-start(f32[64,16,128]{2,0,1:T(8,128)} %copy-done.3), calls=%async_computation.2 | async-start | bytes 983040 | tf_op jit(solution)/shard_map/slice | solution.py:103
  131.2 21.1 %slice-start.1 = ((f32[64,16,128]{2,0,1:T(8,128)}), f32[64,15,128]{2,0,1:T(8,128)S(1)}, s32[]{:S(2)}) async-start(f32[64,16,128]{2,0,1:T(8,128)} %copy-done.4), calls=%async_computation.3 | async-start | bytes 983040 | tf_op jit(solution)/shard_map/slice | solution.py:104
  358.3 27.5 %copy-start.26 = (pred[12]{0:T(512)(128)(4,1)S(1)}, pred[12]{0:T(512)(128)(4,1)}, u32[]{:S(2)}) copy-start(pred[12]{0:T(512)(128)(4,1)} %get-tuple-element.75) | copy-start | bytes 40
  358.3 27.8 %copy-start.30 = (pred[12]{0:T(512)(128)(4,1)S(1)}, pred[12]{0:T(512)(128)(4,1)}, u32[]{:S(2)}) copy-start(pred[12]{0:T(512)(128)(4,1)} %get-tuple-element.80) | copy-start | bytes 40
  360.3 18.3 %collective-permute-start.8 = (bf16[8,2048]{1,0:T(8,128)(2,1)S(1)}, bf16[8,2048]{1,0:T(8,128)(2,1)S(1)}, u32[]{:S(2)}, u32[]{:S(2)}) collective-permute-start(bf16[8,2048]{1,0:T(8,128)(2,1)S(1)} %convolution_convert_fusion.1), channel_id=1, source_target_pairs={{0,24},{8,32},{16,40},{24,48},{32,56},{40,64},{48,72},{56,80},{64,... | collective-permute-start | bytes 98312 | tf_op jit(solution)/shard_map/ppermute | solution.py:14
  362.2 21.1 %collective-permute-start.9 = (bf16[8,2048]{1,0:T(8,128)(2,1)S(1)}, bf16[8,2048]{1,0:T(8,128)(2,1)S(1)}, u32[]{:S(2)}, u32[]{:S(2)}) collective-permute-start(bf16[8,2048]{1,0:T(8,128)(2,1)S(1)} %convolution_convert_fusion.1), channel_id=1, source_target_pairs={{0,16},{8,24},{16,32},{24,40},{32,48},{40,56},{48,64},{56,72},{64,... | collective-permute-start | bytes 98312 | tf_op jit(solution)/shard_map/ppermute | solution.py:14
  364.1 19.2 %collective-permute-start.6 = (bf16[8,2048]{1,0:T(8,128)(2,1)S(1)}, bf16[8,2048]{1,0:T(8,128)(2,1)S(1)}, u32[]{:S(2)}, u32[]{:S(2)}) collective-permute-start(bf16[8,2048]{1,0:T(8,128)(2,1)S(1)} %convolution_convert_fusion.1), channel_id=1, source_target_pairs={{0,8},{8,16},{16,24},{24,32},{32,40},{40,48},{48,56},{56,64},{64,7... | collective-permute-start | bytes 98312 | tf_op jit(solution)/shard_map/ppermute | solution.py:14
  367.7 15.6 %collective-permute-start.7 = (bf16[8,2048]{1,0:T(8,128)(2,1)S(1)}, bf16[8,2048]{1,0:T(8,128)(2,1)S(1)}, u32[]{:S(2)}, u32[]{:S(2)}) collective-permute-start(bf16[8,2048]{1,0:T(8,128)(2,1)S(1)} %convolution_convert_fusion.1), channel_id=1, source_target_pairs={{0,504},{8,0},{16,8},{24,16},{32,24},{40,32},{48,40},{56,48},{64,5... | collective-permute-start | bytes 98312 | tf_op jit(solution)/shard_map/ppermute | solution.py:14
  372.4 11.0 %collective-permute-start.10 = (bf16[8,2048]{1,0:T(8,128)(2,1)S(1)}, bf16[8,2048]{1,0:T(8,128)(2,1)S(1)}, u32[]{:S(2)}, u32[]{:S(2)}) collective-permute-start(bf16[8,2048]{1,0:T(8,128)(2,1)S(1)} %convolution_convert_fusion.1), channel_id=1, source_target_pairs={{0,496},{8,504},{16,0},{24,8},{32,16},{40,24},{48,32},{56,40},{64,... | collective-permute-start | bytes 98312 | tf_op jit(solution)/shard_map/ppermute | solution.py:14
  378.5 6.5 %collective-permute-start.11 = (bf16[8,2048]{1,0:T(8,128)(2,1)S(1)}, bf16[8,2048]{1,0:T(8,128)(2,1)S(1)}, u32[]{:S(2)}, u32[]{:S(2)}) collective-permute-start(bf16[8,2048]{1,0:T(8,128)(2,1)S(1)} %convolution_convert_fusion.1), channel_id=1, source_target_pairs={{0,488},{8,496},{16,504},{24,0},{32,8},{40,16},{48,24},{56,32},{64... | collective-permute-start | bytes 98312 | tf_op jit(solution)/shard_map/ppermute | solution.py:14
  (11 other events, 28.3 us)
Sparse Core Ops, SparseCore 0:
  92.3 75.5 all-gather.1
